TPU v7x, 128 devices: a whole 4x4x4 slice. The times are simulated.
128 devices in a mesh: ctx: 16 (over z, x_lo, core), head: 8 (over y, x_hi).
Axes of the slice: x: 4 (x_hi: 2, x_lo: 2; x = x_hi * 2 + x_lo), y: 4, z: 4, core: 2. Of those that a mesh axis runs over, the one named last changes fastest.
Arguments:
- queries: bfloat16 [24576, 3072], P('ctx', 'head'), may hold values from -160 to 160
- key_states: bfloat16 [24576, 3072], P('ctx', 'head'), may hold values from -12 to 12
- value_states: bfloat16 [24576, 3072], P('ctx', 'head'), may hold values from -18 to 18
- out_grads: bfloat16 [24576, 3072], P(('ctx', 'head')), may hold values from -6 to 6
- pattern: int32 [64, 8], replicated, may hold values from -1 to 63, as said below
Outputs:
- attended: bfloat16 [24576, 3072], P(('ctx', 'head'))
- query_grads: bfloat16 [24576, 3072], P('ctx', 'head')
- key_grads: bfloat16 [24576, 3072], P('ctx', 'head')
- value_grads: bfloat16 [24576, 3072], P('ctx', 'head')
Inputs may be any that keep to these rules, and one draw needn't show every extreme that they name: `pattern`: row t lists distinct tiles whose frame tile (tile // 4) differs from that of t by at most one; t itself is always listed; -1 marks an empty slot and empty slots come last; three or more tiles are listed in every row.
All inputs are finite; a program needn't handle non-finite values.
Results may differ from a plain program's by a relative error of at most 0.035.
Values may be sent and summed in bfloat16 or wider, within the bound.
No kernel may reach another device: no remote copies, remote signals or barrier semaphores. Data moves between devices by JAX's collectives and lax.ppermute only.
A program may use at most 256 MiB of HBM per device.

v0:
```python
import functools
import math

import jax
import jax.numpy as jnp
from jax import lax
from jax.experimental import pallas as pl
from jax.experimental.pallas import tpu as pltpu
from jax.sharding import PartitionSpec as P

HD = 128
TILE = 384
SPT = 4
KSLOT = 8
SCALE = 1.0 / math.sqrt(HD)
NT = (((1,), (1,)), ((), ()))
TN = (((0,), (0,)), ((), ()))


def with_halo(block, axis):
    count = lax.axis_size(axis)
    forward = [(i, i + 1) for i in range(count - 1)]
    backward = [(target, source) for source, target in forward]
    low = lax.ppermute(block, axis, forward)
    high = lax.ppermute(block, axis, backward)
    return (low, block, high)


def from_behind(block, axis, distance):
    devices = range(lax.axis_size(axis))
    route = [(i - distance, i) for i in devices if i - distance in devices]
    return lax.ppermute(block, axis, route)


def lane_fold(x, op):
    parts = [x[:, j * HD : (j + 1) * HD] for j in range(x.shape[1] // HD)]
    return functools.reduce(op, parts)


def pick(slots_ref, a, s, refs):
    slot = slots_ref[a * KSLOT + s]
    region = slot // SPT
    start = pl.multiple_of((slot - region * SPT) * TILE, TILE)
    low, mid, high = (ref[pl.ds(start, TILE), :] for ref in refs)
    return jnp.where(region == 0, low, jnp.where(region == 1, mid, high))


def make_forward_kernel(first):
    def forward_kernel(slots_ref, counts_ref, q_ref, *rest):
        if first:
            k_ref, v_ref, m_ref, l_ref, acc_ref, s_scr = rest

            def key_of(s):
                local = slots_ref[a * KSLOT + s] - SPT
                return k_ref[pl.ds(pl.multiple_of(local * TILE, TILE), TILE), :]

            def value_of(s):
                local = slots_ref[a * KSLOT + s] - SPT
                return v_ref[pl.ds(pl.multiple_of(local * TILE, TILE), TILE), :]
        else:
            (kl_ref, km_ref, kh_ref, vl_ref, vm_ref, vh_ref,
             m_in_ref, l_in_ref, acc_in_ref, o_ref, lse_ref, s_scr) = rest
            key_of = lambda s: pick(slots_ref, a, s, (kl_ref, km_ref, kh_ref))
            value_of = lambda s: pick(slots_ref, a, s, (vl_ref, vm_ref, vh_ref))
        a = pl.program_id(1)
        q = q_ref[...]
        count = counts_ref[a]

        def score_pass(s, row_max):
            scores = lax.dot_general(
                q, key_of(s), NT, preferred_element_type=jnp.float32
            ) * SCALE
            s_scr[s] = scores
            return jnp.maximum(row_max, lane_fold(scores, jnp.maximum))

        init_max = (
            jnp.full((TILE, HD), -jnp.inf, jnp.float32) if first else m_in_ref[...]
        )
        row_max = lax.fori_loop(0, count, score_pass, init_max)
        row_max = jnp.max(row_max, axis=1, keepdims=True)

        def exp_pass(s, carry):
            row_total, acc = carry
            e = jnp.exp(s_scr[s] - row_max)
            acc = acc + jnp.dot(
                e.astype(jnp.bfloat16), value_of(s), preferred_element_type=jnp.float32
            )
            return row_total + lane_fold(e, jnp.add), acc

        if first:
            init = (jnp.zeros((TILE, HD), jnp.float32), jnp.zeros((TILE, HD), jnp.float32))
        else:
            keep = jnp.exp(m_in_ref[:, :1] - row_max)
            init = (l_in_ref[...] * keep, acc_in_ref[...] * keep)
        row_total, acc = lax.fori_loop(0, count, exp_pass, init)
        if first:
            m_ref[...] = jnp.broadcast_to(row_max, (TILE, HD))
            l_ref[...] = row_total
            acc_ref[...] = acc
        else:
            row_total = jnp.sum(row_total, axis=1, keepdims=True)
            o_ref[...] = (acc * (1.0 / row_total)).astype(jnp.bfloat16)
            lse_ref[...] = jnp.broadcast_to(row_max + jnp.log(row_total), (TILE, HD))

    return forward_kernel


def make_backward_kernel(own):
    def backward_kernel(
        slots_ref, counts_ref, q_ref, do_ref, o_ref, lse_ref,
        kl_ref, km_ref, kh_ref, vl_ref, vm_ref, vh_ref, *rest
    ):
        if own:
            dq_in_ref, dq_ref, dk_ref, dv_ref = rest
        else:
            dq_ref, low_ref, high_ref, dk_ref, dv_ref = rest
        a = pl.program_id(1)

        @pl.when(a == 0)
        def _():
            dk_ref[...] = jnp.zeros_like(dk_ref)
            dv_ref[...] = jnp.zeros_like(dv_ref)

        q = q_ref[...]
        do = do_ref[...]
        lse = lse_ref[:, :1]
        delta = jnp.sum(
            do.astype(jnp.float32) * o_ref[...].astype(jnp.float32), axis=1, keepdims=True
        )
        count = counts_ref[a]
        key_of = lambda s: pick(slots_ref, a, s, (kl_ref, km_ref, kh_ref))
        value_of = lambda s: pick(slots_ref, a, s, (vl_ref, vm_ref, vh_ref))

        def acc_rows(s):
            slot = slots_ref[a * KSLOT + s]
            if own:
                slot = slot - SPT
            else:
                slot = jnp.where(slot < SPT, slot, slot - SPT)
            return pl.ds(pl.multiple_of(slot * TILE, TILE), TILE)

        def grad_pass(s, dq_acc):
            ar = acc_rows(s)
            k = key_of(s)
            scores = lax.dot_general(q, k, NT, preferred_element_type=jnp.float32) * SCALE
            w = jnp.exp(scores - lse)
            g = lax.dot_general(do, value_of(s), NT, preferred_element_type=jnp.float32)
            ds = (w * (g - delta)).astype(jnp.bfloat16)
            dk_ref[ar, :] += lax.dot_general(ds, q, TN, preferred_element_type=jnp.float32)
            dv_ref[ar, :] += lax.dot_general(
                w.astype(jnp.bfloat16), do, TN, preferred_element_type=jnp.float32
            )
            return dq_acc + jnp.dot(ds, k, preferred_element_type=jnp.float32)

        init = dq_in_ref[...] if own else jnp.zeros((TILE, HD), jnp.float32)
        dq = lax.fori_loop(0, count, grad_pass, init)
        if own:
            dq_ref[...] = (dq * SCALE).astype(jnp.bfloat16)
        else:
            dq_ref[...] = dq
            half = dk_ref.shape[0] // 2

            @pl.when(a == pl.num_programs(1) - 1)
            def _():
                low_ref[0] = dk_ref[:half, :].astype(jnp.bfloat16)
                low_ref[1] = dv_ref[:half, :].astype(jnp.bfloat16)
                high_ref[0] = dk_ref[half:, :].astype(jnp.bfloat16)
                high_ref[1] = dv_ref[half:, :].astype(jnp.bfloat16)

    return backward_kernel


def specs(row_count, ext_rows):
    tile_spec = pl.BlockSpec((TILE, HD), lambda h, a, sl, ct: (a, h))
    ext_spec = pl.BlockSpec((row_count, HD), lambda h, a, sl, ct: (0, h))
    return tile_spec, ext_spec


def attention_forward(slots, counts, queries, keys, values, carry=None):
    row_count, col_count = queries.shape
    tile_spec, ext_spec = specs(row_count, None)
    first = carry is None
    if first:
        operands = [slots, counts, queries, keys, values]
        in_specs = [tile_spec, ext_spec, ext_spec]
        out_types = [jnp.float32] * 3
    else:
        operands = [slots, counts, queries, *keys, *values, *carry]
        in_specs = [tile_spec] + [ext_spec] * 6 + [tile_spec] * 3
        out_types = [jnp.bfloat16, jnp.float32]
    return pl.pallas_call(
        make_forward_kernel(first),
        grid_spec=pltpu.PrefetchScalarGridSpec(
            num_scalar_prefetch=2,
            grid=(col_count // HD, row_count // TILE),
            in_specs=in_specs,
            out_specs=[tile_spec] * len(out_types),
            scratch_shapes=[pltpu.VMEM((KSLOT, TILE, TILE), jnp.float32)],
        ),
        out_shape=[jax.ShapeDtypeStruct((row_count, col_count), t) for t in out_types],
        compiler_params=pltpu.CompilerParams(
            dimension_semantics=("arbitrary", "arbitrary"),
            vmem_limit_bytes=48 * 1024 * 1024,
        ),
    )(*operands)


def attention_backward(slots, counts, queries, grads, out, lse, keys, values, dq_in=None):
    row_count, col_count = queries.shape
    ext_rows = 3 * row_count
    own = dq_in is not None
    acc_rows = row_count if own else ext_rows - row_count
    tile_spec, ext_spec = specs(row_count, ext_rows)
    acc_spec = pl.BlockSpec((acc_rows, HD), lambda h, a, sl, ct: (0, h))
    operands = [slots, counts, queries, grads, out, lse, *keys, *values]
    in_specs = [tile_spec] * 4 + [ext_spec] * 6
    if own:
        operands.append(dq_in)
        in_specs.append(tile_spec)
    if own:
        out_specs = [tile_spec, acc_spec, acc_spec]
        out_shape = [
            jax.ShapeDtypeStruct((row_count, col_count), jnp.bfloat16),
            jax.ShapeDtypeStruct((acc_rows, col_count), jnp.float32),
            jax.ShapeDtypeStruct((acc_rows, col_count), jnp.float32),
        ]
        scratch = []
    else:
        rim_spec = pl.BlockSpec((2, row_count, HD), lambda h, a, sl, ct: (0, 0, h))
        out_specs = [tile_spec, rim_spec, rim_spec]
        out_shape = [
            jax.ShapeDtypeStruct((row_count, col_count), jnp.float32),
            jax.ShapeDtypeStruct((2, row_count, col_count), jnp.bfloat16),
            jax.ShapeDtypeStruct((2, row_count, col_count), jnp.bfloat16),
        ]
        scratch = [pltpu.VMEM((acc_rows, HD), jnp.float32)] * 2
    return pl.pallas_call(
        make_backward_kernel(own),
        grid_spec=pltpu.PrefetchScalarGridSpec(
            num_scalar_prefetch=2,
            grid=(col_count // HD, row_count // TILE),
            in_specs=in_specs,
            out_specs=out_specs,
            scratch_shapes=scratch,
        ),
        out_shape=out_shape,
        compiler_params=pltpu.CompilerParams(
            dimension_semantics=("arbitrary", "arbitrary"),
            vmem_limit_bytes=48 * 1024 * 1024,
        ),
    )(*operands)


def split_slots(listed, base_tile, first_tile, own_tiles):
    allowed = listed >= 0
    mine = allowed & (listed >= first_tile) & (listed < first_tile + own_tiles)
    near = allowed & ~mine
    slots = jnp.where(allowed, listed - base_tile, 0)
    lists = []
    for keep in (mine, near):
        order = jnp.argsort(~keep, axis=1, stable=True)
        picked = jnp.take_along_axis(slots, order, axis=1)
        lists.append((picked.reshape(-1).astype(jnp.int32), jnp.sum(keep.astype(jnp.int32), axis=1)))
    return lists


def shards(queries, key_states, value_states, out_grads, pattern):
    row_count, col_count = queries.shape
    own_tiles = row_count // TILE
    first_tile = lax.axis_index("ctx") * own_tiles
    base_tile = first_tile - SPT
    keys = with_halo(key_states, "ctx")
    values = with_halo(value_states, "ctx")
    grads_heads = lax.all_to_all(out_grads, "head", split_axis=1, concat_axis=0, tiled=True)
    listed = lax.dynamic_slice_in_dim(pattern, first_tile, own_tiles, 0)
    (own_slots, own_counts), (near_slots, near_counts) = split_slots(
        listed, base_tile, first_tile, own_tiles
    )
    carry = attention_forward(own_slots, own_counts, queries, key_states, value_states)
    out, lse = attention_forward(
        near_slots, near_counts, queries, keys, values, carry
    )
    attended = lax.all_to_all(out, "head", split_axis=0, concat_axis=1, tiled=True)
    dq_part, lower_part, upper_part = attention_backward(
        near_slots, near_counts, queries, grads_heads, out, lse, keys, values
    )
    dq, dk_own, dv_own = attention_backward(
        own_slots, own_counts, queries, grads_heads, out, lse, keys, values, dq_part
    )
    own_part = jnp.stack((dk_own, dv_own))
    from_above = from_behind(lower_part, "ctx", -1).astype(jnp.float32)
    from_below = from_behind(upper_part, "ctx", 1).astype(jnp.float32)
    total = own_part + from_above + from_below
    key_grads = (total[0] * SCALE).astype(jnp.bfloat16)
    value_grads = total[1].astype(jnp.bfloat16)
    return (attended, dq, key_grads, value_grads)


def solution(mesh):
    return jax.shard_map(
        shards,
        mesh=mesh,
        in_specs=(
            P("ctx", "head"),
            P("ctx", "head"),
            P("ctx", "head"),
            P(("ctx", "head"), None),
            P(),
        ),
        out_specs=(P(("ctx", "head"), None), P("ctx", "head"), P("ctx", "head"), P("ctx", "head")),
        check_vma=False,
    )
```

profile of v0, /device:TPU:65, one launch (start us, length us, event | category | flops | bytes accessed | tf_op | source)
XLA Modules:
  0.0 246.0 jit_solution(2753985082285571862)
XLA Ops:
  0.6 3.7 %collective-permute-start = (bf16[1536,384]{1,0:T(8,128)(2,1)}, bf16[1536,384]{1,0:T(8,128)(2,1)}, u32[]{:S(2)}, u32[]{:S(2)}) collective-permute-start(bf16[1536,384]{1,0:T(8,128)(2,1)} %km_ref.3), channel_id=1, source_target_pairs={{0,8},{8,16},{16,24},{24,32},{32,40},{40,48},{48,56},{56,64},{64,7... | collective-permute-start | bytes 3538952 | tf_op jit(solution)/shard_map/ppermute | solution.py:24
  4.3 1.9 collective-permute-start.1
  6.3 3.6 %collective-permute-start.2 = (bf16[1536,384]{1,0:T(8,128)(2,1)}, bf16[1536,384]{1,0:T(8,128)(2,1)}, u32[]{:S(2)}, u32[]{:S(2)}) collective-permute-start(bf16[1536,384]{1,0:T(8,128)(2,1)} %vm_ref.3), channel_id=1, source_target_pairs={{0,8},{8,16},{16,24},{24,32},{32,40},{40,48},{48,56},{56,64},{64,7... | collective-permute-start | bytes 3538952 | tf_op jit(solution)/shard_map/ppermute | solution.py:24
  9.9 1.9 collective-permute-start.3
  11.8 2.4 copy.22
  14.3 6.5 %all-to-all-start.1 = ((bf16[192,8,384]{2,0,1:T(8,128)(2,1)}), bf16[192,8,384]{2,0,1:T(8,128)(2,1)}, u32[]{:S(2)}, u32[]{:S(2)}) async-start(bf16[192,8,384]{2,0,1:T(8,128)(2,1)} %bitcast.24), calls=%async_computation.1 | async-start | bytes 2359296 | tf_op jit(solution)/shard_map/all_to_all | solution.py:274
  23.5 1.3 bitcast_or_fusion
  25.6 1.2 gather_fusion.1
  26.8 1.3 reshape.66
  28.9 1.3 and_select_fusion
  30.2 1.3 copy.16
  32.3 1.3 and_not_fusion
  34.1 1.4 sort.31
  35.5 1.3 clamp_shift-left_fusion.1
  36.8 1.3 copy.11
  38.1 1.3 bitcast_or_fusion.1
  39.4 1.3 reshape.58
  40.6 1.3 gather_fusion
  42.0 1.3 reshape.61
  44.0 1.3 and_select_fusion.1
  45.3 1.3 copy.13
  47.4 23.8 %shard_map.84 = (f32[1536,384]{1,0:T(8,128)S(1)}, f32[1536,384]{1,0:T(8,128)}, f32[1536,384]{1,0:T(8,128)}) custom-call(s32[32]{0:T(128)S(1)} %reshape.33.slots_ref, s32[4]{0:T(128)S(1)} %get-tuple-element.31.counts_ref, bf16[1536,384]{1,0:T(8,128)(2,1)S(1)} %copy-done, bf16[1536,384]{1,0:T(8,128)(2,1)S(1)} %copy-done.1, bf16[1536,384]{1,0:T(8,128)(2,1)S(1)} %copy-done.2), custom_call_target="tpu_custom_call" | custom-call | tf_op jit(solution)/shard_map/pallas_call | solution.py:191
  71.2 1.5 copy-done.3
  72.7 32.3 %shard_map.85 = (bf16[1536,384]{1,0:T(8,128)(2,1)}, f32[1536,384]{1,0:T(8,128)}) custom-call(s32[32]{0:T(128)S(1)} %reshape.32.slots_ref, s32[4]{0:T(128)S(1)} %get-tuple-element.32.counts_ref, bf16[1536,384]{1,0:T(8,128)(2,1)S(1)} %copy-done, bf16[1536,384]{1,0:T(8,128)(2,1)} %collective-permute-done.rest_0_.kl_ref, bf16[1536,384]{1,0:T(8,128)(2,1)S(1)} %copy-done.1, ...), custom_call_target="tpu_custom_call" | custom-call | tf_op jit(solution)/shard_map/pallas_call | solution.py:191
  105.0 36.7 %shard_map.86 = (f32[1536,384]{1,0:T(8,128)}, bf16[2,1536,384]{2,1,0:T(8,128)(2,1)}, bf16[2,1536,384]{2,1,0:T(8,128)(2,1)}) custom-call(s32[32]{0:T(128)S(1)} %reshape.32.slots_ref, s32[4]{0:T(128)S(1)} %get-tuple-element.32.counts_ref, bf16[1536,384]{1,0:T(8,128)(2,1)S(1)} %copy-done, bf16[1536,384]{1,0:T(8,128)(2,1)} %bitcast.5.do_ref, ...), custom_call_target="tpu_custom_call" | custom-call | tf_op jit(solution)/shard_map/pallas_call | solution.py:237
  141.7 27.0 %collective-permute-start.4 = (bf16[2,1536,384]{2,1,0:T(8,128)(2,1)}, bf16[2,1536,384]{2,1,0:T(8,128)(2,1)}, u32[]{:S(2)}, u32[]{:S(2)}) collective-permute-start(bf16[2,1536,384]{2,1,0:T(8,128)(2,1)} %get-tuple-element.29), channel_id=1, source_target_pairs={{8,0},{16,8},{24,16},{32,24},{40,32},{48,40},{56,48},{64,56},{72,6... | collective-permute-start | bytes 7077896 | tf_op jit(solution)/shard_map/ppermute | solution.py:32
  168.8 1.9 collective-permute-start.5
  170.7 6.9 %all-to-all-start = ((bf16[8,192,384]{2,1,0:T(8,128)(2,1)}), bf16[8,192,384]{2,1,0:T(8,128)(2,1)S(1)}, u32[]{:S(2)}, u32[]{:S(2)}) async-start(bf16[8,192,384]{2,1,0:T(8,128)(2,1)} %bitcast.2), calls=%async_computation | async-start | bytes 2359296 | tf_op jit(solution)/shard_map/all_to_all | solution.py:283
  177.6 32.4 %shard_map.87 = (bf16[1536,384]{1,0:T(8,128)(2,1)}, f32[1536,384]{1,0:T(8,128)}, f32[1536,384]{1,0:T(8,128)}) custom-call(s32[32]{0:T(128)S(1)} %reshape.33.slots_ref, s32[4]{0:T(128)S(1)} %get-tuple-element.31.counts_ref, bf16[1536,384]{1,0:T(8,128)(2,1)S(1)} %copy-done, bf16[1536,384]{1,0:T(8,128)(2,1)} %bitcast.5.do_ref, ...), custom_call_target="tpu_custom_call" | custom-call | tf_op jit(solution)/shard_map/pallas_call | solution.py:237
  210.1 28.6 %all-to-all-done = bf16[8,192,384]{2,1,0:T(8,128)(2,1)S(1)} async-done(((bf16[8,192,384]{2,1,0:T(8,128)(2,1)}), bf16[8,192,384]{2,1,0:T(8,128)(2,1)S(1)}, u32[]{:S(2)}, u32[]{:S(2)}) %all-to-all-start) | async-done | bytes 1179680 | tf_op jit(solution)/shard_map/all_to_all | solution.py:283
  239.9 3.7 %fusion = f32[2,1536,384]{2,1,0:T(8,128)S(1)} fusion(f32[1,1536,384]{2,1,0:T(8,128)} %bitcast.27, f32[1,1536,384]{2,1,0:T(8,128)S(1)} %bitcast.26, bf16[2,1536,384]{2,1,0:T(8,128)(2,1)} %collective-permute-done.5, bf16[2,1536,384]{2,1,0:T(8,128)(2,1)} %collective-permute-done.4), kind=kLoop, calls=%fused_computation.3 | loop fusion | flops 5898240 | bytes 14155776 | tf_op jit(solution)/shard_map/add | solution.py:293
  243.6 1.3 fusion.2
  (34 shorter events, 9.6 us)
Async XLA Ops:
  0.6 72.1 %collective-permute-start = (bf16[1536,384]{1,0:T(8,128)(2,1)}, bf16[1536,384]{1,0:T(8,128)(2,1)}, u32[]{:S(2)}, u32[]{:S(2)}) collective-permute-start(bf16[1536,384]{1,0:T(8,128)(2,1)} %km_ref.3), channel_id=1, source_target_pairs={{0,8},{8,16},{16,24},{24,32},{32,40},{40,48},{48,56},{56,64},{64,7... | collective-permute-start | bytes 3538952 | tf_op jit(solution)/shard_map/ppermute | solution.py:24
  4.3 68.4 %collective-permute-start.1 = (bf16[1536,384]{1,0:T(8,128)(2,1)}, bf16[1536,384]{1,0:T(8,128)(2,1)}, u32[]{:S(2)}, u32[]{:S(2)}) collective-permute-start(bf16[1536,384]{1,0:T(8,128)(2,1)} %km_ref.3), channel_id=1, source_target_pairs={{8,0},{16,8},{24,16},{32,24},{40,32},{48,40},{56,48},{64,56},{72,6... | collective-permute-start | bytes 3538952 | tf_op jit(solution)/shard_map/ppermute | solution.py:25
  6.3 66.4 %collective-permute-start.2 = (bf16[1536,384]{1,0:T(8,128)(2,1)}, bf16[1536,384]{1,0:T(8,128)(2,1)}, u32[]{:S(2)}, u32[]{:S(2)}) collective-permute-start(bf16[1536,384]{1,0:T(8,128)(2,1)} %vm_ref.3), channel_id=1, source_target_pairs={{0,8},{8,16},{16,24},{24,32},{32,40},{40,48},{48,56},{56,64},{64,7... | collective-permute-start | bytes 3538952 | tf_op jit(solution)/shard_map/ppermute | solution.py:24
  9.9 62.8 %collective-permute-start.3 = (bf16[1536,384]{1,0:T(8,128)(2,1)}, bf16[1536,384]{1,0:T(8,128)(2,1)}, u32[]{:S(2)}, u32[]{:S(2)}) collective-permute-start(bf16[1536,384]{1,0:T(8,128)(2,1)} %vm_ref.3), channel_id=1, source_target_pairs={{8,0},{16,8},{24,16},{32,24},{40,32},{48,40},{56,48},{64,56},{72,6... | collective-permute-start | bytes 3538952 | tf_op jit(solution)/shard_map/ppermute | solution.py:25
  11.8 8.9 %copy-start.5 = (s32[64,8]{0,1:T(8,128)S(1)}, s32[64,8]{0,1:T(8,128)}, u32[]{:S(2)}) copy-start(s32[64,8]{0,1:T(8,128)} %param.11) | copy-start | bytes 6148
  14.3 90.8 %all-to-all-start.1 = ((bf16[192,8,384]{2,0,1:T(8,128)(2,1)}), bf16[192,8,384]{2,0,1:T(8,128)(2,1)}, u32[]{:S(2)}, u32[]{:S(2)}) async-start(bf16[192,8,384]{2,0,1:T(8,128)(2,1)} %bitcast.24), calls=%async_computation.1 | async-start | bytes 2359296 | tf_op jit(solution)/shard_map/all_to_all | solution.py:274
  20.7 26.7 %copy-start = (bf16[1536,384]{1,0:T(8,128)(2,1)S(1)}, bf16[1536,384]{1,0:T(8,128)(2,1)}, u32[]{:S(2)}) copy-start(bf16[1536,384]{1,0:T(8,128)(2,1)} %q_ref.7) | copy-start | bytes 3538948
  20.7 26.7 %copy-start.1 = (bf16[1536,384]{1,0:T(8,128)(2,1)S(1)}, bf16[1536,384]{1,0:T(8,128)(2,1)}, u32[]{:S(2)}) copy-start(bf16[1536,384]{1,0:T(8,128)(2,1)} %km_ref.3) | copy-start | bytes 3538948
  20.7 26.7 %copy-start.2 = (bf16[1536,384]{1,0:T(8,128)(2,1)S(1)}, bf16[1536,384]{1,0:T(8,128)(2,1)}, u32[]{:S(2)}) copy-start(bf16[1536,384]{1,0:T(8,128)(2,1)} %vm_ref.3) | copy-start | bytes 3538948
  22.0 0.7 copy-start.6
  71.2 1.5 copy-start.3
  141.7 98.1 %collective-permute-start.4 = (bf16[2,1536,384]{2,1,0:T(8,128)(2,1)}, bf16[2,1536,384]{2,1,0:T(8,128)(2,1)}, u32[]{:S(2)}, u32[]{:S(2)}) collective-permute-start(bf16[2,1536,384]{2,1,0:T(8,128)(2,1)} %get-tuple-element.29), channel_id=1, source_target_pairs={{8,0},{16,8},{24,16},{32,24},{40,32},{48,40},{56,48},{64,56},{72,6... | collective-permute-start | bytes 7077896 | tf_op jit(solution)/shard_map/ppermute | solution.py:32
  168.8 71.1 %collective-permute-start.5 = (bf16[2,1536,384]{2,1,0:T(8,128)(2,1)}, bf16[2,1536,384]{2,1,0:T(8,128)(2,1)}, u32[]{:S(2)}, u32[]{:S(2)}) collective-permute-start(bf16[2,1536,384]{2,1,0:T(8,128)(2,1)} %get-tuple-element.30), channel_id=1, source_target_pairs={{0,8},{8,16},{16,24},{24,32},{32,40},{40,48},{48,56},{56,64},{64,7... | collective-permute-start | bytes 7077896 | tf_op jit(solution)/shard_map/ppermute | solution.py:32
  170.7 67.9 %all-to-all-start = ((bf16[8,192,384]{2,1,0:T(8,128)(2,1)}), bf16[8,192,384]{2,1,0:T(8,128)(2,1)S(1)}, u32[]{:S(2)}, u32[]{:S(2)}) async-start(bf16[8,192,384]{2,1,0:T(8,128)(2,1)} %bitcast.2), calls=%async_computation | async-start | bytes 2359296 | tf_op jit(solution)/shard_map/all_to_all | solution.py:283
  210.1 29.8 %copy-start.4 = (f32[1536,384]{1,0:T(8,128)S(1)}, f32[1536,384]{1,0:T(8,128)}, u32[]{:S(2)}) copy-start(f32[1536,384]{1,0:T(8,128)} %get-tuple-element.27) | copy-start | bytes 7077892
where the time goes:
time: 247 us; the launch traced here: 246 us
  Pallas kernels  125 us (51%)
  starting transfers between devices  53.5 us (22%)
  waiting for transfers between devices  28.6 us (12%)
  local copies, waits for them, and re-layouts  21.8 us (9%)
  other arithmetic  16.1 us (7%)
    pallas_call x2, Pallas kernels, attention_backward(): pl.pallas_call(make_backward_kernel(own), grid_spec=pltpu.PrefetchScalarG...  69.1 us
    pallas_call x2, Pallas kernels, attention_forward(): pl.pallas_call(make_forward_kernel(first), grid_spec=pltpu.PrefetchScalar...  56.1 us
    ppermute x2, starting transfers between devices, from_behind(): return lax.ppermute(block, axis, route)  28.9 us
    all_to_all x1, waiting for transfers between devices, shards(): lax.all_to_all(out, 'head', split_axis=0, concat_axis=1, tiled=True)  28.6 us
    gather x10, local copies, waits for them, and re-layouts, split_slots(): picked = jnp.take_along_axis(slots, order, axis=1)  10.7 us
    ppermute x2, starting transfers between devices, with_halo(): low = lax.ppermute(block, axis, forward)  7.33 us
    all_to_all x1, starting transfers between devices, shards(): lax.all_to_all(out, 'head', split_axis=0, concat_axis=1, tiled=True)  6.92 us
    all_to_all x1, starting transfers between devices, shards(): lax.all_to_all(out_grads, 'head', split_axis=1, concat_axis=0, tiled=True)  6.45 us
  transfers between devices with their start and end apart: 8, of which 1 were waited for; matrix products, arithmetic and copies ran while one was open for 12% of the time, Pallas kernels for 36%

commit v1 on v0

--- a/solution.py
+++ b/solution.py
@@ -257,9 +257,11 @@
     near = allowed & ~mine
     slots = jnp.where(allowed, listed - base_tile, 0)
     lists = []
+    places = jnp.arange(listed.shape[1], dtype=jnp.int32)
     for keep in (mine, near):
-        order = jnp.argsort(~keep, axis=1, stable=True)
-        picked = jnp.take_along_axis(slots, order, axis=1)
+        place = jnp.cumsum(keep.astype(jnp.int32), axis=1) - 1
+        hit = keep[:, :, None] & (place[:, :, None] == places[None, None, :])
+        picked = jnp.sum(jnp.where(hit, slots[:, :, None], 0), axis=1)
         lists.append((picked.reshape(-1).astype(jnp.int32), jnp.sum(keep.astype(jnp.int32), axis=1)))
     return lists
 

time: 247 us -> 232 us (0.939)
  the two profiles are of different devices: /device:TPU:65 before, /device:TPU:33 now
where the time goes in v1:
time: 232 us; the launch traced here: 229 us
  Pallas kernels  114 us (49%)
  starting transfers between devices  52.7 us (23%)
  waiting for transfers between devices  37.9 us (16%)
  local copies, waits for them, and re-layouts  13.7 us (6%)
  other arithmetic  10.4 us (4%)
    pallas_call x2, Pallas kernels, attention_backward(): pl.pallas_call(make_backward_kernel(own), grid_spec=pltpu.PrefetchScalarG...  61.8 us
    pallas_call x2, Pallas kernels, attention_forward(): pl.pallas_call(make_forward_kernel(first), grid_spec=pltpu.PrefetchScalar...  51.9 us
    all_to_all x1, waiting for transfers between devices, shards(): lax.all_to_all(out, 'head', split_axis=0, concat_axis=1, tiled=True)  33.8 us
    ppermute x2, starting transfers between devices, from_behind(): return lax.ppermute(block, axis, route)  28.2 us
    ppermute x2, starting transfers between devices, with_halo(): low = lax.ppermute(block, axis, forward)  7.33 us
    all_to_all x1, starting transfers between devices, shards(): lax.all_to_all(out, 'head', split_axis=0, concat_axis=1, tiled=True)  6.94 us
    all_to_all x1, starting transfers between devices, shards(): lax.all_to_all(out_grads, 'head', split_axis=1, concat_axis=0, tiled=True)  6.45 us
  transfers between devices with their start and end apart: 8, of which 2 were waited for; matrix products, arithmetic and copies ran while one was open for 7% of the time, Pallas kernels for 35%

profile of v1, /device:TPU:33, one launch (start us, length us, event | category | flops | bytes accessed | tf_op | source)
XLA Modules:
  0.0 229.2 jit_solution(14696259418854050326)
XLA Ops:
  0.6 3.7 %collective-permute-start = (bf16[1536,384]{1,0:T(8,128)(2,1)}, bf16[1536,384]{1,0:T(8,128)(2,1)}, u32[]{:S(2)}, u32[]{:S(2)}) collective-permute-start(bf16[1536,384]{1,0:T(8,128)(2,1)} %km_ref.3), channel_id=1, source_target_pairs={{0,8},{8,16},{16,24},{24,32},{32,40},{40,48},{48,56},{56,64},{64,7... | collective-permute-start | bytes 3538952 | tf_op jit(solution)/shard_map/ppermute | solution.py:24
  4.3 1.9 collective-permute-start.1
  6.2 3.6 %collective-permute-start.2 = (bf16[1536,384]{1,0:T(8,128)(2,1)}, bf16[1536,384]{1,0:T(8,128)(2,1)}, u32[]{:S(2)}, u32[]{:S(2)}) collective-permute-start(bf16[1536,384]{1,0:T(8,128)(2,1)} %vm_ref.3), channel_id=1, source_target_pairs={{0,8},{8,16},{16,24},{24,32},{32,40},{40,48},{48,56},{56,64},{64,7... | collective-permute-start | bytes 3538952 | tf_op jit(solution)/shard_map/ppermute | solution.py:24
  9.9 1.9 collective-permute-start.3
  11.9 2.6 %copy.26 = bf16[24,8,8,384]{3,2,0,1:T(8,128)(2,1)} copy(bf16[24,8,8,384]{3,2,1,0:T(8,128)(2,1)} %bitcast.21) | data formatting | bytes 2359296 | tf_op jit(solution)/shard_map/all_to_all | solution.py:276
  14.4 6.5 %all-to-all-start.1 = ((bf16[192,8,384]{2,0,1:T(8,128)(2,1)}), bf16[192,8,384]{2,0,1:T(8,128)(2,1)}, u32[]{:S(2)}, u32[]{:S(2)}) async-start(bf16[192,8,384]{2,0,1:T(8,128)(2,1)} %bitcast.17), calls=%async_computation.1 | async-start | bytes 2359296 | tf_op jit(solution)/shard_map/all_to_all | solution.py:276
  21.6 0.6 copy-done.7
  22.1 0.6 convert_element_type.24
  22.7 1.3 copy.16
  24.0 0.7 convert_element_type.25
  24.7 1.3 copy.19
  26.1 1.3 reduce_window_sum.17
  27.4 1.3 broadcast_add_fusion.1
  28.6 1.3 copy.17
  30.0 0.7 copy.18
  30.7 1.4 select_reduce_fusion
  32.1 0.8 reshape.42.slots_ref
  32.9 0.8 reshape.41.slots_ref
  33.7 21.0 %shard_map.84 = (f32[1536,384]{1,0:T(8,128)S(1)}, f32[1536,384]{1,0:T(8,128)}, f32[1536,384]{1,0:T(8,128)}) custom-call(s32[32]{0:T(128)S(1)} %reshape.42.slots_ref, s32[4]{0:T(128)S(1)} %get-tuple-element.28.counts_ref, bf16[1536,384]{1,0:T(8,128)(2,1)S(1)} %copy-done, bf16[1536,384]{1,0:T(8,128)(2,1)S(1)} %copy-done.1, bf16[1536,384]{1,0:T(8,128)(2,1)S(1)} %copy-done.2), custom_call_target="tpu_custom_call" | custom-call | tf_op jit(solution)/shard_map/pallas_call | solution.py:191
  54.6 1.5 copy-done.3
  56.1 4.0 %collective-permute-done.3.rest_5_.vh_ref = bf16[1536,384]{1,0:T(8,128)(2,1)} collective-permute-done((bf16[1536,384]{1,0:T(8,128)(2,1)}, bf16[1536,384]{1,0:T(8,128)(2,1)}, u32[]{:S(2)}, u32[]{:S(2)}) %collective-permute-start.3) | collective-permute-done | bytes 1179680 | tf_op jit(solution)/shard_map/ppermute | solution.py:25
  60.1 31.0 %shard_map.85 = (bf16[1536,384]{1,0:T(8,128)(2,1)}, f32[1536,384]{1,0:T(8,128)}) custom-call(s32[32]{0:T(128)S(1)} %reshape.41.slots_ref, s32[4]{0:T(128)S(1)} %get-tuple-element.31.counts_ref, bf16[1536,384]{1,0:T(8,128)(2,1)S(1)} %copy-done, bf16[1536,384]{1,0:T(8,128)(2,1)} %collective-permute-done.rest_0_.kl_ref, bf16[1536,384]{1,0:T(8,128)(2,1)S(1)} %copy-done.1, ...), custom_call_target="tpu_custom_call" | custom-call | tf_op jit(solution)/shard_map/pallas_call | solution.py:191
  91.0 34.7 %shard_map.86 = (f32[1536,384]{1,0:T(8,128)}, bf16[2,1536,384]{2,1,0:T(8,128)(2,1)}, bf16[2,1536,384]{2,1,0:T(8,128)(2,1)}) custom-call(s32[32]{0:T(128)S(1)} %reshape.41.slots_ref, s32[4]{0:T(128)S(1)} %get-tuple-element.31.counts_ref, bf16[1536,384]{1,0:T(8,128)(2,1)S(1)} %copy-done, bf16[1536,384]{1,0:T(8,128)(2,1)} %bitcast.3.do_ref, ...), custom_call_target="tpu_custom_call" | custom-call | tf_op jit(solution)/shard_map/pallas_call | solution.py:237
  125.7 26.3 %collective-permute-start.4 = (bf16[2,1536,384]{2,1,0:T(8,128)(2,1)}, bf16[2,1536,384]{2,1,0:T(8,128)(2,1)}, u32[]{:S(2)}, u32[]{:S(2)}) collective-permute-start(bf16[2,1536,384]{2,1,0:T(8,128)(2,1)} %get-tuple-element.24), channel_id=1, source_target_pairs={{8,0},{16,8},{24,16},{32,24},{40,32},{48,40},{56,48},{64,56},{72,6... | collective-permute-start | bytes 7077896 | tf_op jit(solution)/shard_map/ppermute | solution.py:32
  152.0 1.9 collective-permute-start.5
  153.9 6.9 %all-to-all-start = ((bf16[8,192,384]{2,1,0:T(8,128)(2,1)}), bf16[8,192,384]{2,1,0:T(8,128)(2,1)S(1)}, u32[]{:S(2)}, u32[]{:S(2)}) async-start(bf16[8,192,384]{2,1,0:T(8,128)(2,1)} %bitcast), calls=%async_computation | async-start | bytes 2359296 | tf_op jit(solution)/shard_map/all_to_all | solution.py:285
  160.8 27.2 %shard_map.87 = (bf16[1536,384]{1,0:T(8,128)(2,1)}, f32[1536,384]{1,0:T(8,128)}, f32[1536,384]{1,0:T(8,128)}) custom-call(s32[32]{0:T(128)S(1)} %reshape.42.slots_ref, s32[4]{0:T(128)S(1)} %get-tuple-element.28.counts_ref, bf16[1536,384]{1,0:T(8,128)(2,1)S(1)} %copy-done, bf16[1536,384]{1,0:T(8,128)(2,1)} %bitcast.3.do_ref, ...), custom_call_target="tpu_custom_call" | custom-call | tf_op jit(solution)/shard_map/pallas_call | solution.py:237
  188.0 33.8 %all-to-all-done = bf16[8,192,384]{2,1,0:T(8,128)(2,1)S(1)} async-done(((bf16[8,192,384]{2,1,0:T(8,128)(2,1)}), bf16[8,192,384]{2,1,0:T(8,128)(2,1)S(1)}, u32[]{:S(2)}, u32[]{:S(2)}) %all-to-all-start) | async-done | bytes 1179680 | tf_op jit(solution)/shard_map/all_to_all | solution.py:285
  221.8 1.2 copy.24
  223.1 3.7 %fusion = f32[2,1536,384]{2,1,0:T(8,128)S(1)} fusion(f32[1,1536,384]{2,1,0:T(8,128)} %bitcast.20, f32[1,1536,384]{2,1,0:T(8,128)S(1)} %bitcast.19, bf16[2,1536,384]{2,1,0:T(8,128)(2,1)} %collective-permute-done.5, bf16[2,1536,384]{2,1,0:T(8,128)(2,1)} %collective-permute-done.4), kind=kLoop, calls=%fused_computation.1 | loop fusion | flops 5898240 | bytes 14155776 | tf_op jit(solution)/shard_map/add | solution.py:295
  226.8 1.3 fusion.2
  228.0 1.1 fusion.3
  (25 shorter events, 0.8 us)
Async XLA Ops:
  0.6 55.4 %collective-permute-start = (bf16[1536,384]{1,0:T(8,128)(2,1)}, bf16[1536,384]{1,0:T(8,128)(2,1)}, u32[]{:S(2)}, u32[]{:S(2)}) collective-permute-start(bf16[1536,384]{1,0:T(8,128)(2,1)} %km_ref.3), channel_id=1, source_target_pairs={{0,8},{8,16},{16,24},{24,32},{32,40},{40,48},{48,56},{56,64},{64,7... | collective-permute-start | bytes 3538952 | tf_op jit(solution)/shard_map/ppermute | solution.py:24
  4.3 51.8 %collective-permute-start.1 = (bf16[1536,384]{1,0:T(8,128)(2,1)}, bf16[1536,384]{1,0:T(8,128)(2,1)}, u32[]{:S(2)}, u32[]{:S(2)}) collective-permute-start(bf16[1536,384]{1,0:T(8,128)(2,1)} %km_ref.3), channel_id=1, source_target_pairs={{8,0},{16,8},{24,16},{32,24},{40,32},{48,40},{56,48},{64,56},{72,6... | collective-permute-start | bytes 3538952 | tf_op jit(solution)/shard_map/ppermute | solution.py:25
  6.2 49.8 %collective-permute-start.2 = (bf16[1536,384]{1,0:T(8,128)(2,1)}, bf16[1536,384]{1,0:T(8,128)(2,1)}, u32[]{:S(2)}, u32[]{:S(2)}) collective-permute-start(bf16[1536,384]{1,0:T(8,128)(2,1)} %vm_ref.3), channel_id=1, source_target_pairs={{0,8},{8,16},{16,24},{24,32},{32,40},{40,48},{48,56},{56,64},{64,7... | collective-permute-start | bytes 3538952 | tf_op jit(solution)/shard_map/ppermute | solution.py:24
  9.9 50.2 %collective-permute-start.3 = (bf16[1536,384]{1,0:T(8,128)(2,1)}, bf16[1536,384]{1,0:T(8,128)(2,1)}, u32[]{:S(2)}, u32[]{:S(2)}) collective-permute-start(bf16[1536,384]{1,0:T(8,128)(2,1)} %vm_ref.3), channel_id=1, source_target_pairs={{8,0},{16,8},{24,16},{32,24},{40,32},{48,40},{56,48},{64,56},{72,6... | collective-permute-start | bytes 3538952 | tf_op jit(solution)/shard_map/ppermute | solution.py:25
  11.8 9.1 %copy-start.5 = (s32[64,8]{0,1:T(8,128)S(1)}, s32[64,8]{0,1:T(8,128)}, u32[]{:S(2)}) copy-start(s32[64,8]{0,1:T(8,128)} %param.9) | copy-start | bytes 6148
  11.8 21.8 %copy-start = (bf16[1536,384]{1,0:T(8,128)(2,1)S(1)}, bf16[1536,384]{1,0:T(8,128)(2,1)}, u32[]{:S(2)}) copy-start(bf16[1536,384]{1,0:T(8,128)(2,1)} %q_ref.7) | copy-start | bytes 3538948
  11.9 21.8 %copy-start.1 = (bf16[1536,384]{1,0:T(8,128)(2,1)S(1)}, bf16[1536,384]{1,0:T(8,128)(2,1)}, u32[]{:S(2)}) copy-start(bf16[1536,384]{1,0:T(8,128)(2,1)} %km_ref.3) | copy-start | bytes 3538948
  11.9 21.8 %copy-start.2 = (bf16[1536,384]{1,0:T(8,128)(2,1)S(1)}, bf16[1536,384]{1,0:T(8,128)(2,1)}, u32[]{:S(2)}) copy-start(bf16[1536,384]{1,0:T(8,128)(2,1)} %vm_ref.3) | copy-start | bytes 3538948
  14.4 76.6 %all-to-all-start.1 = ((bf16[192,8,384]{2,0,1:T(8,128)(2,1)}), bf16[192,8,384]{2,0,1:T(8,128)(2,1)}, u32[]{:S(2)}, u32[]{:S(2)}) async-start(bf16[192,8,384]{2,0,1:T(8,128)(2,1)} %bitcast.17), calls=%async_computation.1 | async-start | bytes 2359296 | tf_op jit(solution)/shard_map/all_to_all | solution.py:276
  21.0 0.6 copy-start.6
  21.6 0.6 copy-start.7
  54.6 1.5 copy-start.3
  125.7 97.4 %collective-permute-start.4 = (bf16[2,1536,384]{2,1,0:T(8,128)(2,1)}, bf16[2,1536,384]{2,1,0:T(8,128)(2,1)}, u32[]{:S(2)}, u32[]{:S(2)}) collective-permute-start(bf16[2,1536,384]{2,1,0:T(8,128)(2,1)} %get-tuple-element.24), channel_id=1, source_target_pairs={{8,0},{16,8},{24,16},{32,24},{40,32},{48,40},{56,48},{64,56},{72,6... | collective-permute-start | bytes 7077896 | tf_op jit(solution)/shard_map/ppermute | solution.py:32
  152.0 71.1 %collective-permute-start.5 = (bf16[2,1536,384]{2,1,0:T(8,128)(2,1)}, bf16[2,1536,384]{2,1,0:T(8,128)(2,1)}, u32[]{:S(2)}, u32[]{:S(2)}) collective-permute-start(bf16[2,1536,384]{2,1,0:T(8,128)(2,1)} %get-tuple-element.25), channel_id=1, source_target_pairs={{0,8},{8,16},{16,24},{24,32},{32,40},{40,48},{48,56},{56,64},{64,7... | collective-permute-start | bytes 7077896 | tf_op jit(solution)/shard_map/ppermute | solution.py:32
  153.9 68.0 %all-to-all-start = ((bf16[8,192,384]{2,1,0:T(8,128)(2,1)}), bf16[8,192,384]{2,1,0:T(8,128)(2,1)S(1)}, u32[]{:S(2)}, u32[]{:S(2)}) async-start(bf16[8,192,384]{2,1,0:T(8,128)(2,1)} %bitcast), calls=%async_computation | async-start | bytes 2359296 | tf_op jit(solution)/shard_map/all_to_all | solution.py:285
  188.0 35.1 %copy-start.4 = (f32[1536,384]{1,0:T(8,128)S(1)}, f32[1536,384]{1,0:T(8,128)}, u32[]{:S(2)}) copy-start(f32[1536,384]{1,0:T(8,128)} %get-tuple-element.22) | copy-start | bytes 7077892
